TPU v7x, 256 devices: a whole 4x4x8 slice. The times are simulated.
256 devices in a mesh: seq: 16 (over y, z_hi, core), head: 16 (over x, z_lo).
Axes of the slice: x: 4, y: 4, z: 8 (z_hi: 2, z_lo: 4; z = z_hi * 4 + z_lo), core: 2. Of those that a mesh axis runs over, the one named last changes fastest.
Arguments:
- x_in: bfloat16 [8192, 8192], P('seq', 'head'), may hold values from -6 to 6
- z_in: bfloat16 [8192, 8192], P('seq', 'head'), may hold values from -12 to 12
- bc: bfloat16 [2, 8192, 128], P(None, 'seq'), may hold values from -1.796875 to 1.796875
- dt_raw: float32 [128, 8192], P('head', 'seq'), may hold values from -3 to 3
- dt_bias: float32 [128], P('head'), may hold values from -8 to 0
- decay_rate: float32 [128], P('head'), may hold values from 0.001 to 0.4
- d_skip: float32 [128], P('head'), may hold values from 0.5 to 1.5
- norm_gain: float32 [8192], P('head'), may hold values from 0.1 to 1.9
- out_weight: bfloat16 [8192, 4096], P('head', 'seq'), may hold values from -0.0625 to 0.0625
- resid: bfloat16 [8192, 4096], P(('seq', 'head')), may hold values from -6 to 6
- mlp_gain: float32 [4096], replicated, may hold values from 0.1 to 1.9
- gate_weight: bfloat16 [4096, 8192], P(None, 'head'), may hold values from -0.09375 to 0.09375
- up_weight: bfloat16 [4096, 8192], P(None, 'head'), may hold values from -0.09375 to 0.09375
- down_weight: bfloat16 [8192, 4096], P('head', 'seq'), may hold values from -0.0625 to 0.0625
Outputs:
- layer_out: bfloat16 [8192, 4096], P(('seq', 'head'))
All inputs are finite; a program needn't handle non-finite values.
Results may differ from a plain program's by a relative error of at most 0.0075.
Values may be sent and summed in bfloat16 or wider, within the bound.
No kernel may reach another device: no remote copies, remote signals or barrier semaphores. Data moves between devices by JAX's collectives and lax.ppermute only.
A program may use at most 128 MiB of HBM per device.

v0:
```python
import jax
import jax.numpy as jnp
from jax import lax
from jax.sharding import PartitionSpec as P

BLOCK = 256
INNER = 8192
epsilon = 1e-05
SEQ = ("sy", "sz", "sc")


def block_scan(x_heads, b_rows, c_rows, step_size, log_decay, block_len):
    length, head_count, head_width = x_heads.shape
    state_size = b_rows.shape[1]
    block_count = length // block_len
    lower_mask = jnp.tril(jnp.ones((block_len, block_len), dtype=bool))
    carry_state = jnp.zeros((head_count, head_width, state_size), jnp.float32)
    outs = []
    for blk in range(block_count):
        rows = slice(blk * block_len, (blk + 1) * block_len)
        x_block = x_heads[rows]
        b_block = b_rows[rows]
        c_block = c_rows[rows]
        d_block = step_size[:, rows]
        a_block = log_decay[:, rows]
        cumulative = jnp.cumsum(a_block, axis=1)
        gap_values = jnp.where(
            lower_mask[None], cumulative[:, :, None] - cumulative[:, None, :], -jnp.inf
        )
        scores = jnp.dot(c_block, b_block.T, preferred_element_type=jnp.float32)
        mixing = (jnp.exp(gap_values) * scores[None] * d_block[:, None, :]).astype(jnp.bfloat16)
        within = jnp.einsum("hij,jhp->ihp", mixing, x_block, preferred_element_type=jnp.float32)
        if blk > 0:
            carried = jnp.einsum(
                "in,hpn->ihp",
                c_block.astype(jnp.float32),
                carry_state,
                precision=lax.Precision.HIGHEST,
            )
            within = within + carried * jnp.exp(cumulative).T[:, :, None]
        last_cum = cumulative[:, -1:]
        inject = (
            (jnp.exp(last_cum - cumulative) * d_block)[:, :, None]
            * b_block.astype(jnp.float32)[None]
        ).astype(jnp.bfloat16)
        added = jnp.einsum("jhp,hjn->hpn", x_block, inject, preferred_element_type=jnp.float32)
        carry_state = jnp.exp(last_cum)[:, :, None] * carry_state + added
        outs.append(within)
    return (jnp.concatenate(outs, axis=0), carry_state)


def combine(first, second):
    (d1, s1), (d2, s2) = (first, second)
    return (d1 * d2, d2[:, None, None] * s1 + s2)


def send(pair, pairs, axes):
    return tuple((lax.ppermute(v, axes, pairs) for v in pair))


def entering_state(group_decay, local_state):
    block = ("sz", "sc")
    j = lax.axis_index("sz") * 2 + lax.axis_index("sc")
    y = lax.axis_index("sy")
    ny = lax.axis_size("sy")
    own = (group_decay, local_state)
    ident = (jnp.ones_like(group_decay), jnp.zeros_like(local_state))

    def pick(cond, a, b):
        return tuple((jnp.where(cond, u, v) for u, v in zip(a, b)))

    got = send(own, [(0, 1), (2, 3)], block)
    pair_agg = combine(got, own)
    lower = send(pair_agg, [(1, 2)], block)
    lower3 = send(lower, [(2, 3)], block)
    inner = pick(j == 1, got, ident)
    inner = pick(j == 2, lower, inner)
    inner = pick(j == 3, combine(lower3, got), inner)
    block_agg = combine(lower3, pair_agg)
    full = SEQ
    before = ident
    for k in range(ny - 1, 0, -1):
        pairs = [(4 * src + 3, 4 * (src + k) + 3) for src in range(ny - k)]
        got_k = send(block_agg, pairs, full)
        before = combine(before, pick(y >= k, got_k, ident))
    to_2 = send(before, [(3, 2)], block)
    to_1 = send(before, [(3, 1)], block)
    to_0 = send(to_1, [(1, 0)], block)
    prefix = pick(j == 3, before, to_0)
    prefix = pick(j == 2, to_2, prefix)
    prefix = pick(j == 1, to_1, prefix)
    return combine(prefix, inner)[1]


def ring_sum_x(pieces):
    nx = pieces.shape[0]
    x = lax.axis_index("hx")
    half = pieces.shape[2] // 2
    ways = ((1, pieces[:, :, :half]), (-1, pieces[:, :, half:]))
    accs = []
    for way, part in ways:
        pairs = [(src, (src + way) % nx) for src in range(nx)]
        acc = jnp.take(part, (x - way) % nx, axis=0).astype(jnp.float32)
        for step in range(nx - 1):
            got = lax.ppermute(acc.astype(jnp.bfloat16), "hx", pairs)
            chunk = (x - way * (step + 2)) % nx
            acc = got.astype(jnp.float32) + jnp.take(part, chunk, axis=0).astype(jnp.float32)
        accs.append(acc)
    return jnp.concatenate(accs, axis=1)


def sum_over_head(value):
    nx, nz = (lax.axis_size("hx"), lax.axis_size("hz"))
    pieces = value.reshape(nx, nz, value.shape[0] // (nx * nz), value.shape[1])
    pieces = ring_sum_x(pieces).astype(jnp.bfloat16)
    pieces = lax.all_to_all(pieces, "hz", 0, 0, tiled=False)
    return jnp.sum(pieces.astype(jnp.float32), axis=0)


def ring_gather_x(value):
    nx = lax.axis_size("hx")
    x = lax.axis_index("hx")
    half = value.shape[0] // 2
    slots = jnp.arange(nx)
    outs = []
    for way, part in ((1, value[:half]), (-1, value[half:])):
        pairs = [(src, (src + way) % nx) for src in range(nx)]
        got = [part]
        for step in range(nx - 1):
            got.append(lax.ppermute(got[-1], "hx", pairs))
        stacked = jnp.stack(got)
        outs.append(jnp.take(stacked, way * (x - slots) % nx, axis=0))
    return jnp.concatenate(outs, axis=1).reshape(nx * value.shape[0], value.shape[1])


def gather_z(value):
    nz = lax.axis_size("hz")
    copies = jnp.broadcast_to(value[None], (nz,) + value.shape)
    got = lax.all_to_all(copies, "hz", 0, 0, tiled=False)
    return got.reshape(nz * value.shape[0], value.shape[1])


def gather_over_head(value):
    return ring_gather_x(gather_z(value))


def normalize_rows(layer_sum, mlp_gain):
    mean_square = jnp.mean(layer_sum * layer_sum, axis=1, keepdims=True)
    return (layer_sum * lax.rsqrt(mean_square + epsilon) * mlp_gain).astype(jnp.bfloat16)


def shards(
    x_in,
    z_in,
    bc,
    dt_raw,
    dt_bias,
    decay_rate,
    d_skip,
    norm_gain,
    out_weight,
    resid,
    mlp_gain,
    gate_weight,
    up_weight,
    down_weight,
):
    out_full, down_full = (
        lax.all_gather(out_weight, SEQ, axis=1, tiled=True),
        lax.all_gather(down_weight, SEQ, axis=1, tiled=True),
    )
    head_count = dt_raw.shape[0]
    length = dt_raw.shape[1]
    head_width = x_in.shape[1] // head_count
    step_size = jax.nn.softplus(dt_raw + dt_bias[:, None])
    log_decay = -decay_rate[:, None] * step_size
    x_heads = x_in.reshape(length, head_count, head_width)
    local_out, local_state = block_scan(x_heads, bc[0], bc[1], step_size, log_decay, BLOCK)
    running = jnp.cumsum(log_decay, axis=1)
    group_decay = jnp.exp(running[:, -1])
    entering = entering_state(group_decay, local_state)
    carried = jnp.einsum(
        "tn,hpn->thp", bc[1].astype(jnp.float32), entering, precision=lax.Precision.HIGHEST
    )
    carried = carried * jnp.exp(running).T[:, :, None]
    ssd_out = local_out + carried + d_skip[None, :, None] * x_heads.astype(jnp.float32)
    gated_out = ssd_out.reshape(length, head_count * head_width) * jax.nn.silu(
        z_in.astype(jnp.float32)
    )
    row_squares = jnp.sum(gated_out * gated_out, axis=1)
    gated_scaled = (gated_out * norm_gain).astype(jnp.bfloat16)
    head_n = lax.axis_size("hx") * lax.axis_size("hz")
    chunks = 1
    rows_per = length // head_n // chunks
    width = out_full.shape[1]
    gated_parts = gated_scaled.reshape(head_n, chunks, rows_per, -1)
    square_parts = row_squares.reshape(head_n, chunks, rows_per)
    resid_parts = resid.reshape(chunks, rows_per, -1)

    def packed_rows(chunk):
        chunk_rows = gated_parts[:, chunk].reshape(head_n * rows_per, -1)
        chunk_squares = square_parts[:, chunk].reshape(head_n * rows_per)
        partial_value = jnp.dot(chunk_rows, out_full, preferred_element_type=jnp.float32)
        sq_hi = chunk_squares.astype(jnp.bfloat16)
        sq_lo = (chunk_squares - sq_hi.astype(jnp.float32)).astype(jnp.bfloat16)
        extra = (
            jnp.zeros((head_n * rows_per, 128), jnp.bfloat16)
            .at[:, 0]
            .set(sq_hi)
            .at[:, 1]
            .set(sq_lo)
        )
        return jnp.concatenate([partial_value.astype(jnp.bfloat16), extra], axis=1)

    def finish_rows(reduced, chunk):
        part_rows = reduced[:, :width]
        part_squares = reduced[:, width] + reduced[:, width + 1]
        layer_sum = (
            resid_parts[chunk].astype(jnp.float32)
            + part_rows * lax.rsqrt(part_squares / INNER + epsilon)[:, None]
        )
        return (layer_sum, normalize_rows(layer_sum, mlp_gain))

    def mlp_rows(rows_piece, down_full):
        gate_part = jnp.dot(rows_piece, gate_weight, preferred_element_type=jnp.float32)
        up_part = jnp.dot(rows_piece, up_weight, preferred_element_type=jnp.float32)
        hidden = (jax.nn.silu(gate_part) * up_part).astype(jnp.bfloat16)
        mlp_part = jnp.dot(hidden, down_full, preferred_element_type=jnp.float32)
        return sum_over_head(mlp_part.astype(jnp.bfloat16))

    packs = [packed_rows(chunk) for chunk in range(chunks)]
    normed_rows = []
    sums = []
    for chunk in range(chunks):
        pack = packs[chunk]
        if chunk > 0:
            pack, normed_rows[-1] = lax.optimization_barrier((pack, normed_rows[-1]))
        reduced = sum_over_head(pack)
        if chunk == 0:
            reduced, down_full = lax.optimization_barrier((reduced, down_full))
        layer_sum, normed = finish_rows(reduced, chunk)
        sums.append(layer_sum)
        normed_rows.append(normed)
    gathered = []
    for chunk in range(chunks):
        gathered.append(gather_over_head(normed_rows[chunk]))
        if chunk + 1 < chunks:
            gathered[-1], normed_rows[chunk + 1] = lax.optimization_barrier(
                (gathered[-1], normed_rows[chunk + 1])
            )
    outs = [sums[c] + mlp_rows(gathered[c], down_full) for c in range(chunks)]
    return jnp.concatenate(outs, axis=0).astype(jnp.bfloat16)


def solution(mesh):
    seq_n, head_n = mesh.devices.shape
    devices = mesh.devices.reshape(seq_n // 4, 2, 2, 4, head_n // 4)
    mesh = jax.sharding.Mesh(devices, ("sy", "sz", "sc", "hx", "hz"))
    head = ("hx", "hz")
    in_specs = (
        P(SEQ, head),
        P(SEQ, head),
        P(None, SEQ, None),
        P(head, SEQ),
        P(head),
        P(head),
        P(head),
        P(head),
        P(head, SEQ),
        P(SEQ + head, None),
        P(),
        P(None, head),
        P(None, head),
        P(head, SEQ),
    )
    out_specs = P(SEQ + head, None)
    return jax.shard_map(shards, mesh=mesh, in_specs=in_specs, out_specs=out_specs, check_vma=False)
```

profile of v0, /device:TPU:8, one launch (start us, length us, event | category | flops | bytes accessed | tf_op | source)
XLA Modules:
  0.0 354.5 jit_solution(17849686165738651231)
XLA Ops:
  6.5 0.7 all-gather.3.cloned.1.call-update
  8.0 0.8 broadcast_multiply_fusion
  10.3 1.1 fusion.73
  13.2 1.8 collective-permute-start.6
  15.0 1.1 reduce-window.26
  16.6 1.3 collective-permute-start
  17.9 0.9 fusion.53
  18.9 0.8 collective-permute-start.7
  20.0 1.2 fusion.5
  21.9 0.7 collective-permute-start.2
  22.6 0.7 collective-permute-start.8
  23.3 0.7 collective-permute-start.5
  23.9 0.7 collective-permute-start.4
  24.6 0.7 collective-permute-start.3
  25.4 0.7 collective-permute-start.11
  26.1 0.7 collective-permute-start.10
  26.8 0.7 collective-permute-start.9
  27.7 0.7 collective-permute-start.12
  28.8 0.7 compare_reduce_fusion.1
  29.5 0.7 compare_reduce_fusion
  30.3 1.8 convolution_bitcast_fusion.3
  32.0 0.8 collective-permute-start.13
  32.9 1.3 collective-permute-start.14
  34.2 0.7 fusion.4
  34.9 38.6 %collective-permute-done.14 = f32[8,64,128]{2,1,0:T(8,128)S(1)} collective-permute-done((f32[8,64,128]{2,1,0:T(8,128)S(1)}, f32[8,64,128]{2,1,0:T(8,128)S(1)}, u32[]{:S(2)}, u32[]{:S(2)}) %collective-permute-start.14) | collective-permute-done | bytes 262176 | tf_op jit(solution)/shard_map/ppermute | solution.py:58
  73.5 0.8 fusion.2
  74.7 0.7 copy-done.5
  76.0 1.4 fusion.40
  77.8 18.0 %all-gather.3.cloned.1.call-done = bf16[512,4096]{1,0:T(8,128)(2,1)} async-done(((bf16[512,256]{1,0:T(8,128)(2,1)}), bf16[512,4096]{1,0:T(8,128)(2,1)}) %all-gather.3.cloned.1.call-update) | async-done | bytes 4194320 | tf_op jit(solution)/shard_map/all_gather | solution.py:169
  95.8 4.6 %convolution_convert_fusion.1 = bf16[512,4096]{1,0:T(8,128)(2,1)S(1)} fusion(bf16[512,4096]{1,0:T(8,128)(2,1)} %all-gather.3.cloned.1.call-done, f32[512]{0:T(512)S(1)} %copy-done.16, f32[512,512]{1,0:T(8,128)S(1)} %copy.29, bf16[512,512]{1,0:T(8,128)(2,1)S(1)} %copy-done.5), kind=kOutput, calls=%fused_computation.3 | convolution fusion | flops 2151677952 | bytes 9963520 | tf_op jit(solution)/shard_map/dot_general | solution.py:203
  101.2 2.8 collective-permute-start.18
  104.3 11.6 %collective-permute-done.18 = bf16[4,16,4224]{2,1,0:T(8,128)(2,1)S(1)} collective-permute-done((bf16[4,16,4224]{2,1,0:T(8,128)(2,1)S(1)}, bf16[4,16,4224]{2,1,0:T(8,128)(2,1)S(1)}, u32[]{:S(2)}, u32[]{:S(2)}) %collective-permute-start.18) | collective-permute-done | bytes 540704 | tf_op jit(solution)/shard_map/ppermute | solution.py:105
  116.1 3.8 %collective-permute-start.19 = (bf16[4,16,4224]{2,1,0:T(8,128)(2,1)S(1)}, bf16[4,16,4224]{2,1,0:T(8,128)(2,1)S(1)}, u32[]{:S(2)}, u32[]{:S(2)}) collective-permute-start(bf16[4,16,4224]{2,1,0:T(8,128)(2,1)S(1)} %add_convert_fusion.2), channel_id=1, source_target_pairs={{0,12},{4,0},{8,4},{12,8},{1,13},{5,1},{9,5},{13,9},{2,14},{6,2},{... | collective-permute-start | bytes 1622024 | tf_op jit(solution)/shard_map/ppermute | solution.py:105
  120.1 10.8 %collective-permute-done.19 = bf16[4,16,4224]{2,1,0:T(8,128)(2,1)S(1)} collective-permute-done((bf16[4,16,4224]{2,1,0:T(8,128)(2,1)S(1)}, bf16[4,16,4224]{2,1,0:T(8,128)(2,1)S(1)}, u32[]{:S(2)}, u32[]{:S(2)}) %collective-permute-start.19) | collective-permute-done | bytes 540704 | tf_op jit(solution)/shard_map/ppermute | solution.py:105
  131.1 3.8 %collective-permute-start.20 = (bf16[4,16,4224]{2,1,0:T(8,128)(2,1)S(1)}, bf16[4,16,4224]{2,1,0:T(8,128)(2,1)S(1)}, u32[]{:S(2)}, u32[]{:S(2)}) collective-permute-start(bf16[4,16,4224]{2,1,0:T(8,128)(2,1)S(1)} %add_convert_fusion.1), channel_id=1, source_target_pairs={{0,12},{4,0},{8,4},{12,8},{1,13},{5,1},{9,5},{13,9},{2,14},{6,2},{... | collective-permute-start | bytes 1622024 | tf_op jit(solution)/shard_map/ppermute | solution.py:105
  135.2 10.0 %collective-permute-done.20 = bf16[4,16,4224]{2,1,0:T(8,128)(2,1)S(1)} collective-permute-done((bf16[4,16,4224]{2,1,0:T(8,128)(2,1)S(1)}, bf16[4,16,4224]{2,1,0:T(8,128)(2,1)S(1)}, u32[]{:S(2)}, u32[]{:S(2)}) %collective-permute-start.20) | collective-permute-done | bytes 540704 | tf_op jit(solution)/shard_map/ppermute | solution.py:105
  145.3 3.5 collective-permute-done.17
  149.1 34.4 %all_to_all.15 = bf16[4,32,4224]{2,1,0:T(8,128)(2,1)S(1)} all-to-all(bf16[4,32,4224]{2,1,0:T(8,128)(2,1)S(1)} %pad_maximum_fusion.4), channel_id=1, replica_groups=mesh['sy'=4,'sz'=2,'sc'=2,'hx'=4,'hz'=4] {'hz'}, dimensions={0} | all-to-all | bytes 2162688 | tf_op jit(solution)/shard_map/all_to_all | solution.py:116
  184.4 29.2 %all_to_all.16 = bf16[4,32,4096]{2,1,0:T(8,128)(2,1)S(1)} all-to-all(bf16[4,32,4096]{2,1,0:T(8,128)(2,1)S(1)} %broadcast_in_dim.42), channel_id=1, replica_groups=mesh['sy'=4,'sz'=2,'sc'=2,'hx'=4,'hz'=4] {'hz'}, dimensions={0} | all-to-all | bytes 2097152 | tf_op jit(solution)/shard_map/all_to_all | solution.py:139
  213.7 3.3 collective-permute-start.24
  217.0 10.5 %collective-permute-done.24 = bf16[64,4096]{1,0:T(8,128)(2,1)S(1)} collective-permute-done((bf16[64,4096]{1,0:T(8,128)(2,1)S(1)}, bf16[64,4096]{1,0:T(8,128)(2,1)S(1)}, u32[]{:S(2)}, u32[]{:S(2)}) %collective-permute-start.24) | collective-permute-done | bytes 524320 | tf_op jit(solution)/shard_map/ppermute | solution.py:130
  227.5 3.7 %collective-permute-start.25 = (bf16[64,4096]{1,0:T(8,128)(2,1)S(1)}, bf16[64,4096]{1,0:T(8,128)(2,1)S(1)}, u32[]{:S(2)}, u32[]{:S(2)}) collective-permute-start(bf16[64,4096]{1,0:T(8,128)(2,1)S(1)} %collective-permute-done.24), channel_id=1, source_target_pairs={{0,12},{4,0},{8,4},{12,8},{1,13},{5,1},{9,5},{13,9},{2,14},{6,2},{... | collective-permute-start | bytes 1572872 | tf_op jit(solution)/shard_map/ppermute | solution.py:130
  231.2 9.6 %collective-permute-done.25 = bf16[64,4096]{1,0:T(8,128)(2,1)S(1)} collective-permute-done((bf16[64,4096]{1,0:T(8,128)(2,1)S(1)}, bf16[64,4096]{1,0:T(8,128)(2,1)S(1)}, u32[]{:S(2)}, u32[]{:S(2)}) %collective-permute-start.25) | collective-permute-done | bytes 524320 | tf_op jit(solution)/shard_map/ppermute | solution.py:130
  240.8 3.7 %collective-permute-start.26 = (bf16[64,4096]{1,0:T(8,128)(2,1)S(1)}, bf16[64,4096]{1,0:T(8,128)(2,1)S(1)}, u32[]{:S(2)}, u32[]{:S(2)}) collective-permute-start(bf16[64,4096]{1,0:T(8,128)(2,1)S(1)} %collective-permute-done.25), channel_id=1, source_target_pairs={{0,12},{4,0},{8,4},{12,8},{1,13},{5,1},{9,5},{13,9},{2,14},{6,2},{... | collective-permute-start | bytes 1572872 | tf_op jit(solution)/shard_map/ppermute | solution.py:130
  244.9 8.4 %collective-permute-done.26 = bf16[64,4096]{1,0:T(8,128)(2,1)S(1)} collective-permute-done((bf16[64,4096]{1,0:T(8,128)(2,1)S(1)}, bf16[64,4096]{1,0:T(8,128)(2,1)S(1)}, u32[]{:S(2)}, u32[]{:S(2)}) %collective-permute-start.26) | collective-permute-done | bytes 524320 | tf_op jit(solution)/shard_map/ppermute | solution.py:130
  253.5 2.0 gather_fusion.1
  255.5 3.2 broadcast_select_fusion
  258.8 1.5 pad_maximum_fusion.2
  260.2 2.0 gather_fusion
  262.3 2.0 broadcast_select_fusion.1
  265.0 2.1 copy-done.1
  267.1 1.1 copy-done.15
  268.2 2.3 fusion.74
  270.5 11.2 %convolution_convert_fusion = bf16[512,4096]{1,0:T(8,128)(2,1)} fusion(bf16[512,4096]{1,0:T(8,128)(2,1)} %all-gather.5.cloned.1.call-done, bf16[512,4096]{1,0:T(8,128)(2,1)} %bitcast.126, bf16[4096,512]{1,0:T(8,128)(2,1)} %param.36, f32[512,512]{1,0:T(8,128)S(1)} %fusion.74), kind=kOutput, calls=%fused_computation.2 | convolution fusion | flops 4298637312 | bytes 17825792 | tf_op jit(solution)/shard_map/dot_general | solution.py:228
  281.7 2.7 fusion.71
  284.5 3.8 %collective-permute-start.30 = (bf16[4,16,4096]{2,1,0:T(8,128)(2,1)S(1)}, bf16[4,16,4096]{2,1,0:T(8,128)(2,1)S(1)}, u32[]{:S(2)}, u32[]{:S(2)}) collective-permute-start(bf16[4,16,4096]{2,1,0:T(8,128)(2,1)S(1)} %select_bitcast_fusion.2), channel_id=1, source_target_pairs={{0,12},{4,0},{8,4},{12,8},{1,13},{5,1},{9,5},{13,9},{2,14},{6,2},{... | collective-permute-start | bytes 1572872 | tf_op jit(solution)/shard_map/ppermute | solution.py:105
  288.5 8.0 %collective-permute-done.30 = bf16[4,16,4096]{2,1,0:T(8,128)(2,1)S(1)} collective-permute-done((bf16[4,16,4096]{2,1,0:T(8,128)(2,1)S(1)}, bf16[4,16,4096]{2,1,0:T(8,128)(2,1)S(1)}, u32[]{:S(2)}, u32[]{:S(2)}) %collective-permute-start.30) | collective-permute-done | bytes 524320 | tf_op jit(solution)/shard_map/ppermute | solution.py:105
  296.6 3.8 %collective-permute-start.31 = (bf16[4,16,4096]{2,1,0:T(8,128)(2,1)S(1)}, bf16[4,16,4096]{2,1,0:T(8,128)(2,1)S(1)}, u32[]{:S(2)}, u32[]{:S(2)}) collective-permute-start(bf16[4,16,4096]{2,1,0:T(8,128)(2,1)S(1)} %add_convert_fusion.8), channel_id=1, source_target_pairs={{0,12},{4,0},{8,4},{12,8},{1,13},{5,1},{9,5},{13,9},{2,14},{6,2},{... | collective-permute-start | bytes 1572872 | tf_op jit(solution)/shard_map/ppermute | solution.py:105
  300.6 7.9 %collective-permute-done.31 = bf16[4,16,4096]{2,1,0:T(8,128)(2,1)S(1)} collective-permute-done((bf16[4,16,4096]{2,1,0:T(8,128)(2,1)S(1)}, bf16[4,16,4096]{2,1,0:T(8,128)(2,1)S(1)}, u32[]{:S(2)}, u32[]{:S(2)}) %collective-permute-start.31) | collective-permute-done | bytes 524320 | tf_op jit(solution)/shard_map/ppermute | solution.py:105
  308.7 3.8 %collective-permute-start.32 = (bf16[4,16,4096]{2,1,0:T(8,128)(2,1)S(1)}, bf16[4,16,4096]{2,1,0:T(8,128)(2,1)S(1)}, u32[]{:S(2)}, u32[]{:S(2)}) collective-permute-start(bf16[4,16,4096]{2,1,0:T(8,128)(2,1)S(1)} %add_convert_fusion.7), channel_id=1, source_target_pairs={{0,12},{4,0},{8,4},{12,8},{1,13},{5,1},{9,5},{13,9},{2,14},{6,2},{... | collective-permute-start | bytes 1572872 | tf_op jit(solution)/shard_map/ppermute | solution.py:105
  312.7 6.4 %collective-permute-done.32 = bf16[4,16,4096]{2,1,0:T(8,128)(2,1)S(1)} collective-permute-done((bf16[4,16,4096]{2,1,0:T(8,128)(2,1)S(1)}, bf16[4,16,4096]{2,1,0:T(8,128)(2,1)S(1)}, u32[]{:S(2)}, u32[]{:S(2)}) %collective-permute-start.32) | collective-permute-done | bytes 524320 | tf_op jit(solution)/shard_map/ppermute | solution.py:105
  319.3 3.8 %collective-permute-done.29 = bf16[4,16,4096]{2,1,0:T(8,128)(2,1)S(1)} collective-permute-done((bf16[4,16,4096]{2,1,0:T(8,128)(2,1)S(1)}, bf16[4,16,4096]{2,1,0:T(8,128)(2,1)S(1)}, u32[]{:S(2)}, u32[]{:S(2)}) %collective-permute-start.29) | collective-permute-done | bytes 524320 | tf_op jit(solution)/shard_map/ppermute | solution.py:105
  323.4 23.3 %all_to_all.17 = bf16[4,32,4096]{2,1,0:T(8,128)(2,1)S(1)} all-to-all(bf16[4,32,4096]{2,1,0:T(8,128)(2,1)S(1)} %pad_maximum_fusion.5), channel_id=1, replica_groups=mesh['sy'=4,'sz'=2,'sc'=2,'hx'=4,'hz'=4] {'hz'}, dimensions={0} | all-to-all | bytes 2097152 | tf_op jit(solution)/shard_map/all_to_all | solution.py:116
  346.8 0.8 add_convert_fusion.12
  (141 shorter events, 13.5 us)
Async XLA Ops:
  6.5 5.6 %copy-start.4 = (bf16[2,512,128]{2,1,0:T(8,128)(2,1)S(1)}, bf16[2,512,128]{2,1,0:T(8,128)(2,1)}, u32[]{:S(2)}) copy-start(bf16[2,512,128]{2,1,0:T(8,128)(2,1)} %param.26) | copy-start | bytes 786436
  6.5 89.2 %all-gather.3.cloned.1.call-start = ((), (), s32[]{:S(2)}) async-start(), calls=%async_computation.3 | async-start | bytes 4456448 | tf_op jit(solution)/shard_map/all_gather | solution.py:169
  7.3 176.4 %all-gather.5.cloned.1.call-start = ((), (), s32[]{:S(2)}) async-start(), calls=%async_computation.4 | async-start | bytes 4456448 | tf_op jit(solution)/shard_map/all_gather | solution.py:170
  11.7 1.0 copy-start.9
  13.2 5.6 %collective-permute-start.6 = (f32[8,64,128]{2,1,0:T(8,128)S(1)}, f32[8,64,128]{2,1,0:T(8,128)S(1)}, u32[]{:S(2)}, u32[]{:S(2)}) collective-permute-start(f32[8,64,128]{2,1,0:T(8,128)S(1)} %fusion.6), channel_id=1, source_target_pairs={{0,16},{32,48},{1,17},{33,49},{2,18},{34,50},{3,19},{35,51},{4,20}... | collective-permute-start | bytes 786440 | tf_op jit(solution)/shard_map/ppermute | solution.py:58
  16.6 4.6 %collective-permute-start = (f32[8]{0:T(128)S(1)}, f32[8]{0:T(128)S(1)}, u32[]{:S(2)}, u32[]{:S(2)}) collective-permute-start(f32[8]{0:T(128)S(1)} %fusion.61), channel_id=1, source_target_pairs={{0,16},{32,48},{1,17},{33,49},{2,18},{34,50},{3,19},{35,51},{4,20}... | collective-permute-start | bytes 104 | tf_op jit(solution)/shard_map/ppermute | solution.py:58
  18.8 9.7 %copy-start.3 = (bf16[512,512]{1,0:T(8,128)(2,1)S(1)}, bf16[512,512]{1,0:T(8,128)(2,1)}, u32[]{:S(2)}) copy-start(bf16[512,512]{1,0:T(8,128)(2,1)} %param.24) | copy-start | bytes 1572868
  18.9 3.6 %collective-permute-start.7 = (f32[8,64,128]{2,1,0:T(8,128)S(1)}, f32[8,64,128]{2,1,0:T(8,128)S(1)}, u32[]{:S(2)}, u32[]{:S(2)}) collective-permute-start(f32[8,64,128]{2,1,0:T(8,128)S(1)} %multiply_add_fusion.2), channel_id=1, source_target_pairs={{16,32},{17,33},{18,34},{19,35},{20,36},{21,37},{22,38},{23,39},{2... | collective-permute-start | bytes 786440 | tf_op jit(solution)/shard_map/ppermute | solution.py:58
  21.2 0.7 collective-permute-start.1
  21.9 1.4 collective-permute-start.2
  22.5 6.0 %copy-start.10 = (f32[8,64,128]{2,1,0:T(8,128)}, f32[8,64,128]{2,1,0:T(8,128)S(1)}, u32[]{:S(2)}) copy-start(f32[8,64,128]{2,1,0:T(8,128)S(1)} %collective-permute-done.7) | copy-start | bytes 786436
  22.6 2.7 collective-permute-start.8
  23.3 2.0 collective-permute-start.5
  23.9 3.5 collective-permute-start.4
  24.6 2.9 collective-permute-start.3
  25.4 2.1 collective-permute-start.11
  26.1 1.4 collective-permute-start.10
  26.8 0.8 collective-permute-start.9
  27.7 5.2 %collective-permute-start.12 = (f32[8,64,128]{2,1,0:T(8,128)S(1)}, f32[8,64,128]{2,1,0:T(8,128)S(1)}, u32[]{:S(2)}, u32[]{:S(2)}) collective-permute-start(f32[8,64,128]{2,1,0:T(8,128)S(1)} %select_add_fusion), channel_id=1, source_target_pairs={{48,16},{49,17},{50,18},{51,19},{52,20},{53,21},{54,22},{55,23},{5... | collective-permute-start | bytes 786440 | tf_op jit(solution)/shard_map/ppermute | solution.py:58
  28.8 5.4 %copy-start.6 = (f32[256,8,64]{0,2,1:T(8,128)S(1)}, f32[256,8,64]{0,2,1:T(8,128)}, u32[]{:S(2)}) copy-start(f32[256,8,64]{0,2,1:T(8,128)} %fusion.5) | copy-start | bytes 1572868
  32.0 41.5 %copy-start.11 = (f32[8,64,128]{2,1,0:T(8,128)S(1)}, f32[8,64,128]{2,1,0:T(8,128)}, u32[]{:S(2)}) copy-start(f32[8,64,128]{2,1,0:T(8,128)} %copy-done.10) | copy-start | bytes 786436
  32.0 41.5 %copy-start.14 = (f32[8]{0:T(128)S(1)}, f32[8]{0:T(128)}, u32[]{:S(2)}) copy-start(f32[8]{0:T(128)} %param.30) | copy-start | bytes 100
  32.0 2.9 collective-permute-start.13
  32.9 40.7 %copy-start.12 = (f32[8,64,128]{2,1,0:T(8,128)}, f32[8,64,128]{2,1,0:T(8,128)S(1)}, u32[]{:S(2)}) copy-start(f32[8,64,128]{2,1,0:T(8,128)S(1)} %collective-permute-done.12) | copy-start | bytes 786436
  32.9 40.7 %collective-permute-start.14 = (f32[8,64,128]{2,1,0:T(8,128)S(1)}, f32[8,64,128]{2,1,0:T(8,128)S(1)}, u32[]{:S(2)}, u32[]{:S(2)}) collective-permute-start(f32[8,64,128]{2,1,0:T(8,128)S(1)} %collective-permute-done.12), channel_id=1, source_target_pairs={{16,0},{17,1},{18,2},{19,3},{20,4},{21,5},{22,6},{23,7},{24,8},{25... | collective-permute-start | bytes 786440 | tf_op jit(solution)/shard_map/ppermute | solution.py:58
  74.3 1.0 copy-start.5
  74.3 21.4 %copy-start.16 = (f32[512]{0:T(512)S(1)}, f32[512]{0:T(512)}, u32[]{:S(2)}) copy-start(f32[512]{0:T(512)} %param.31) | copy-start | bytes 6148
  101.2 14.7 %collective-permute-start.18 = (bf16[4,16,4224]{2,1,0:T(8,128)(2,1)S(1)}, bf16[4,16,4224]{2,1,0:T(8,128)(2,1)S(1)}, u32[]{:S(2)}, u32[]{:S(2)}) collective-permute-start(bf16[4,16,4224]{2,1,0:T(8,128)(2,1)S(1)} %select_bitcast_fusion), channel_id=1, source_target_pairs={{0,12},{4,0},{8,4},{12,8},{1,13},{5,1},{9,5},{13,9},{2,14},{6,2},{... | collective-permute-start | bytes 1622024 | tf_op jit(solution)/shard_map/ppermute | solution.py:105
  104.0 15.8 %collective-permute-start.15 = (bf16[4,16,4224]{2,1,0:T(8,128)(2,1)S(1)}, bf16[4,16,4224]{2,1,0:T(8,128)(2,1)S(1)}, u32[]{:S(2)}, u32[]{:S(2)}) collective-permute-start(bf16[4,16,4224]{2,1,0:T(8,128)(2,1)S(1)} %select_bitcast_fusion.1), channel_id=1, source_target_pairs={{0,4},{4,8},{8,12},{12,0},{1,5},{5,9},{9,13},{13,1},{2,6},{6,10},{... | collective-permute-start | bytes 1622024 | tf_op jit(solution)/shard_map/ppermute | solution.py:105
  116.1 14.9 %collective-permute-start.19 = (bf16[4,16,4224]{2,1,0:T(8,128)(2,1)S(1)}, bf16[4,16,4224]{2,1,0:T(8,128)(2,1)S(1)}, u32[]{:S(2)}, u32[]{:S(2)}) collective-permute-start(bf16[4,16,4224]{2,1,0:T(8,128)(2,1)S(1)} %add_convert_fusion.2), channel_id=1, source_target_pairs={{0,12},{4,0},{8,4},{12,8},{1,13},{5,1},{9,5},{13,9},{2,14},{6,2},{... | collective-permute-start | bytes 1622024 | tf_op jit(solution)/shard_map/ppermute | solution.py:105
  120.0 14.9 %collective-permute-start.16 = (bf16[4,16,4224]{2,1,0:T(8,128)(2,1)S(1)}, bf16[4,16,4224]{2,1,0:T(8,128)(2,1)S(1)}, u32[]{:S(2)}, u32[]{:S(2)}) collective-permute-start(bf16[4,16,4224]{2,1,0:T(8,128)(2,1)S(1)} %add_convert_fusion.5), channel_id=1, source_target_pairs={{0,4},{4,8},{8,12},{12,0},{1,5},{5,9},{9,13},{13,1},{2,6},{6,10},{... | collective-permute-start | bytes 1622024 | tf_op jit(solution)/shard_map/ppermute | solution.py:105
  131.1 14.0 %collective-permute-start.20 = (bf16[4,16,4224]{2,1,0:T(8,128)(2,1)S(1)}, bf16[4,16,4224]{2,1,0:T(8,128)(2,1)S(1)}, u32[]{:S(2)}, u32[]{:S(2)}) collective-permute-start(bf16[4,16,4224]{2,1,0:T(8,128)(2,1)S(1)} %add_convert_fusion.1), channel_id=1, source_target_pairs={{0,12},{4,0},{8,4},{12,8},{1,13},{5,1},{9,5},{13,9},{2,14},{6,2},{... | collective-permute-start | bytes 1622024 | tf_op jit(solution)/shard_map/ppermute | solution.py:105
  135.1 13.7 %collective-permute-start.17 = (bf16[4,16,4224]{2,1,0:T(8,128)(2,1)S(1)}, bf16[4,16,4224]{2,1,0:T(8,128)(2,1)S(1)}, u32[]{:S(2)}, u32[]{:S(2)}) collective-permute-start(bf16[4,16,4224]{2,1,0:T(8,128)(2,1)S(1)} %add_convert_fusion.4), channel_id=1, source_target_pairs={{0,4},{4,8},{8,12},{12,0},{1,5},{5,9},{9,13},{13,1},{2,6},{6,10},{... | collective-permute-start | bytes 1622024 | tf_op jit(solution)/shard_map/ppermute | solution.py:105
  149.1 34.8 %copy-start.2 = (bf16[32,4096]{1,0:T(8,128)(2,1)S(1)}, bf16[32,4096]{1,0:T(8,128)(2,1)}, u32[]{:S(2)}) copy-start(bf16[32,4096]{1,0:T(8,128)(2,1)} %param.33) | copy-start | bytes 786436
  149.1 35.0 %copy-start.13 = (f32[4096]{0:T(1024)S(1)}, f32[4096]{0:T(1024)}, u32[]{:S(2)}) copy-start(f32[4096]{0:T(1024)} %param.34) | copy-start | bytes 49156
  213.7 13.8 %collective-permute-start.24 = (bf16[64,4096]{1,0:T(8,128)(2,1)S(1)}, bf16[64,4096]{1,0:T(8,128)(2,1)S(1)}, u32[]{:S(2)}, u32[]{:S(2)}) collective-permute-start(bf16[64,4096]{1,0:T(8,128)(2,1)S(1)} %bitcast.131), channel_id=1, source_target_pairs={{0,12},{4,0},{8,4},{12,8},{1,13},{5,1},{9,5},{13,9},{2,14},{6,2},{... | collective-permute-start | bytes 1572872 | tf_op jit(solution)/shard_map/ppermute | solution.py:130
  217.0 14.2 %collective-permute-start.21 = (bf16[64,4096]{1,0:T(8,128)(2,1)S(1)}, bf16[64,4096]{1,0:T(8,128)(2,1)S(1)}, u32[]{:S(2)}, u32[]{:S(2)}) collective-permute-start(bf16[64,4096]{1,0:T(8,128)(2,1)S(1)} %bitcast.129), channel_id=1, source_target_pairs={{0,4},{4,8},{8,12},{12,0},{1,5},{5,9},{9,13},{13,1},{2,6},{6,10},{... | collective-permute-start | bytes 1572872 | tf_op jit(solution)/shard_map/ppermute | solution.py:130
  227.5 13.3 %collective-permute-start.25 = (bf16[64,4096]{1,0:T(8,128)(2,1)S(1)}, bf16[64,4096]{1,0:T(8,128)(2,1)S(1)}, u32[]{:S(2)}, u32[]{:S(2)}) collective-permute-start(bf16[64,4096]{1,0:T(8,128)(2,1)S(1)} %collective-permute-done.24), channel_id=1, source_target_pairs={{0,12},{4,0},{8,4},{12,8},{1,13},{5,1},{9,5},{13,9},{2,14},{6,2},{... | collective-permute-start | bytes 1572872 | tf_op jit(solution)/shard_map/ppermute | solution.py:130
  231.2 22.1 %copy-start.7 = (bf16[64,4096]{1,0:T(8,128)(2,1)}, bf16[64,4096]{1,0:T(8,128)(2,1)S(1)}, u32[]{:S(2)}) copy-start(bf16[64,4096]{1,0:T(8,128)(2,1)S(1)} %collective-permute-done.21) | copy-start | bytes 1572868
  231.2 13.4 %collective-permute-start.22 = (bf16[64,4096]{1,0:T(8,128)(2,1)S(1)}, bf16[64,4096]{1,0:T(8,128)(2,1)}, u32[]{:S(2)}, u32[]{:S(2)}) collective-permute-start(bf16[64,4096]{1,0:T(8,128)(2,1)S(1)} %collective-permute-done.21), channel_id=1, source_target_pairs={{0,4},{4,8},{8,12},{12,0},{1,5},{5,9},{9,13},{13,1},{2,6},{6,10},{... | collective-permute-start | bytes 1572872 | tf_op jit(solution)/shard_map/ppermute | solution.py:130
  240.8 12.5 %collective-permute-start.26 = (bf16[64,4096]{1,0:T(8,128)(2,1)S(1)}, bf16[64,4096]{1,0:T(8,128)(2,1)S(1)}, u32[]{:S(2)}, u32[]{:S(2)}) collective-permute-start(bf16[64,4096]{1,0:T(8,128)(2,1)S(1)} %collective-permute-done.25), channel_id=1, source_target_pairs={{0,12},{4,0},{8,4},{12,8},{1,13},{5,1},{9,5},{13,9},{2,14},{6,2},{... | collective-permute-start | bytes 1572872 | tf_op jit(solution)/shard_map/ppermute | solution.py:130
  244.6 14.2 %collective-permute-start.23 = (bf16[64,4096]{1,0:T(8,128)(2,1)}, bf16[64,4096]{1,0:T(8,128)(2,1)}, u32[]{:S(2)}, u32[]{:S(2)}) collective-permute-start(bf16[64,4096]{1,0:T(8,128)(2,1)} %collective-permute-done.22), channel_id=1, source_target_pairs={{0,4},{4,8},{8,12},{12,0},{1,5},{5,9},{9,13},{13,1},{2,6},{6,10},{... | collective-permute-start | bytes 1572872 | tf_op jit(solution)/shard_map/ppermute | solution.py:130
  255.5 3.2 copy-start.8
  262.3 2.2 copy-start
  264.5 3.7 %copy-start.15 = (bf16[4096,512]{1,0:T(8,128)(2,1)S(1)}, bf16[4096,512]{1,0:T(8,128)(2,1)}, u32[]{:S(2)}) copy-start(bf16[4096,512]{1,0:T(8,128)(2,1)} %param.35) | copy-start | bytes 12582916
  265.0 2.1 copy-start.1
  284.5 11.9 %collective-permute-start.30 = (bf16[4,16,4096]{2,1,0:T(8,128)(2,1)S(1)}, bf16[4,16,4096]{2,1,0:T(8,128)(2,1)S(1)}, u32[]{:S(2)}, u32[]{:S(2)}) collective-permute-start(bf16[4,16,4096]{2,1,0:T(8,128)(2,1)S(1)} %select_bitcast_fusion.2), channel_id=1, source_target_pairs={{0,12},{4,0},{8,4},{12,8},{1,13},{5,1},{9,5},{13,9},{2,14},{6,2},{... | collective-permute-start | bytes 1572872 | tf_op jit(solution)/shard_map/ppermute | solution.py:105
  288.4 12.0 %collective-permute-start.27 = (bf16[4,16,4096]{2,1,0:T(8,128)(2,1)S(1)}, bf16[4,16,4096]{2,1,0:T(8,128)(2,1)S(1)}, u32[]{:S(2)}, u32[]{:S(2)}) collective-permute-start(bf16[4,16,4096]{2,1,0:T(8,128)(2,1)S(1)} %select_bitcast_fusion.3), channel_id=1, source_target_pairs={{0,4},{4,8},{8,12},{12,0},{1,5},{5,9},{9,13},{13,1},{2,6},{6,10},{... | collective-permute-start | bytes 1572872 | tf_op jit(solution)/shard_map/ppermute | solution.py:105
  296.6 11.9 %collective-permute-start.31 = (bf16[4,16,4096]{2,1,0:T(8,128)(2,1)S(1)}, bf16[4,16,4096]{2,1,0:T(8,128)(2,1)S(1)}, u32[]{:S(2)}, u32[]{:S(2)}) collective-permute-start(bf16[4,16,4096]{2,1,0:T(8,128)(2,1)S(1)} %add_convert_fusion.8), channel_id=1, source_target_pairs={{0,12},{4,0},{8,4},{12,8},{1,13},{5,1},{9,5},{13,9},{2,14},{6,2},{... | collective-permute-start | bytes 1572872 | tf_op jit(solution)/shard_map/ppermute | solution.py:105
  300.6 11.9 %collective-permute-start.28 = (bf16[4,16,4096]{2,1,0:T(8,128)(2,1)S(1)}, bf16[4,16,4096]{2,1,0:T(8,128)(2,1)S(1)}, u32[]{:S(2)}, u32[]{:S(2)}) collective-permute-start(bf16[4,16,4096]{2,1,0:T(8,128)(2,1)S(1)} %add_convert_fusion.11), channel_id=1, source_target_pairs={{0,4},{4,8},{8,12},{12,0},{1,5},{5,9},{9,13},{13,1},{2,6},{6,10},{... | collective-permute-start | bytes 1572872 | tf_op jit(solution)/shard_map/ppermute | solution.py:105
  308.7 10.5 %collective-permute-start.32 = (bf16[4,16,4096]{2,1,0:T(8,128)(2,1)S(1)}, bf16[4,16,4096]{2,1,0:T(8,128)(2,1)S(1)}, u32[]{:S(2)}, u32[]{:S(2)}) collective-permute-start(bf16[4,16,4096]{2,1,0:T(8,128)(2,1)S(1)} %add_convert_fusion.7), channel_id=1, source_target_pairs={{0,12},{4,0},{8,4},{12,8},{1,13},{5,1},{9,5},{13,9},{2,14},{6,2},{... | collective-permute-start | bytes 1572872 | tf_op jit(solution)/shard_map/ppermute | solution.py:105
  312.6 10.5 %collective-permute-start.29 = (bf16[4,16,4096]{2,1,0:T(8,128)(2,1)S(1)}, bf16[4,16,4096]{2,1,0:T(8,128)(2,1)S(1)}, u32[]{:S(2)}, u32[]{:S(2)}) collective-permute-start(bf16[4,16,4096]{2,1,0:T(8,128)(2,1)S(1)} %add_convert_fusion.10), channel_id=1, source_target_pairs={{0,4},{4,8},{8,12},{12,0},{1,5},{5,9},{9,13},{13,1},{2,6},{6,10},{... | collective-permute-start | bytes 1572872 | tf_op jit(solution)/shard_map/ppermute | solution.py:105
Sparse Core Ops, SparseCore 0:
  9.9 85.8 all-gather.2
  98.3 78.7 all-gather.4
where the time goes:
time: 355 us; the launch traced here: 354 us
  waiting for transfers between devices  148 us (42%)
  blocking collectives  86.8 us (24%)
  starting transfers between devices  46 us (13%)
  matrix products  24.8 us (7%)
  other arithmetic  20 us (6%)
  local copies, waits for them, and re-layouts  14.6 us (4%)
  between operations  14.5 us (4%)
    ppermute x12, waiting for transfers between devices, ring_sum_x(): got = lax.ppermute(acc.astype(jnp.bfloat16), 'hx', pairs)  62.1 us
    all_to_all x2, blocking collectives, sum_over_head(): pieces = lax.all_to_all(pieces, 'hz', 0, 0, tiled=False)  57.6 us
    ppermute x15, waiting for transfers between devices, send(): return tuple((lax.ppermute(v, axes, pairs) for v in pair))  38.6 us
    all_to_all x1, blocking collectives, gather_z(): got = lax.all_to_all(copies, 'hz', 0, 0, tiled=False)  29.2 us
    ppermute x6, waiting for transfers between devices, ring_gather_x(): got.append(lax.ppermute(got[-1], 'hx', pairs))  28.5 us
    ppermute x12, starting transfers between devices, ring_sum_x(): got = lax.ppermute(acc.astype(jnp.bfloat16), 'hx', pairs)  22.3 us
    all_gather x1, waiting for transfers between devices, shards(): lax.all_gather(out_weight, SEQ, axis=1, tiled=True)  18 us
    ppermute x15, starting transfers between devices, send(): return tuple((lax.ppermute(v, axes, pairs) for v in pair))  12.6 us
  transfers between devices with their start and end apart: 35, of which 13 were waited for; matrix products, arithmetic and copies ran while one was open for 9% of the time, Pallas kernels for 0%

commit v1 on v0

--- a/solution.py
+++ b/solution.py
@@ -2,11 +2,21 @@
 import jax.numpy as jnp
 from jax import lax
 from jax.sharding import PartitionSpec as P
+from jax.lax import all_to_all, axis_size
 
 BLOCK = 256
 INNER = 8192
 epsilon = 1e-05
 SEQ = ("sy", "sz", "sc")
+shape_roots = lambda array_here, axis_k: jnp.concatenate(
+    all_to_all(
+        jnp.stack([array_here for _ in range(axis_size(SEQ))], axis=0),
+        axis_name=SEQ,
+        split_axis=0,
+        concat_axis=0,
+    ),
+    axis=axis_k,
+)
 
 
 def block_scan(x_heads, b_rows, c_rows, step_size, log_decay, block_len):
@@ -166,7 +176,7 @@
     down_weight,
 ):
     out_full, down_full = (
-        lax.all_gather(out_weight, SEQ, axis=1, tiled=True),
+        shape_roots(out_weight, 1),
         lax.all_gather(down_weight, SEQ, axis=1, tiled=True),
     )
     head_count = dt_raw.shape[0]

time: 355 us -> 434 us (1.22)
  waiting for transfers between devices: 148 us -> 197 us
  blocking collectives: 86.8 us -> 104 us
  starting transfers between devices: 46 us -> 53.7 us
    ppermute x15, waiting for transfers between devices: 38.6 us -> 103 us  [send(): return tuple((lax.ppermute(v, axes, pairs) for v in pair))]
    all_to_all x2, blocking collectives: 57.6 us -> 76.7 us  [sum_over_head(): pieces = lax.all_to_all(pieces, 'hz', 0, 0, tiled=False)]
    all_gather x1 -> x0, waiting for transfers between devices: 18 us -> none  [shards(): lax.all_gather(out_weight, SEQ, axis=1, tiled=True)]
    all_to_all x0 -> x1, starting transfers between devices: none -> 11.7 us  [all_to_all(jnp.stack([array_here for _ in range(axis_size(SEQ))], axis=0)...]
  transfers between devices with their start and end apart: 35 -> 35, of which waited for: 13 -> 13; matrix products, arithmetic and copies ran while one was open for 9% -> 7% of each run, Pallas kernels for 0% -> 0%
where the time goes in v1:
time: 434 us; the launch traced here: 429 us
  waiting for transfers between devices  197 us (45%)
  blocking collectives  104 us (24%)
  starting transfers between devices  53.7 us (12%)
  matrix products  24.8 us (6%)
  other arithmetic  18.5 us (4%)
  local copies, waits for them, and re-layouts  17 us (4%)
  between operations  14.5 us (3%)
    ppermute x15, waiting for transfers between devices, send(): return tuple((lax.ppermute(v, axes, pairs) for v in pair))  103 us
    all_to_all x2, blocking collectives, sum_over_head(): pieces = lax.all_to_all(pieces, 'hz', 0, 0, tiled=False)  76.7 us
    ppermute x12, waiting for transfers between devices, ring_sum_x(): got = lax.ppermute(acc.astype(jnp.bfloat16), 'hx', pairs)  65 us
    ppermute x6, waiting for transfers between devices, ring_gather_x(): got.append(lax.ppermute(got[-1], 'hx', pairs))  28.2 us
    all_to_all x1, blocking collectives, gather_z(): got = lax.all_to_all(copies, 'hz', 0, 0, tiled=False)  27.5 us
    ppermute x12, starting transfers between devices, ring_sum_x(): got = lax.ppermute(acc.astype(jnp.bfloat16), 'hx', pairs)  22.2 us
    ppermute x15, starting transfers between devices, send(): return tuple((lax.ppermute(v, axes, pairs) for v in pair))  12.8 us
    all_to_all x1, starting transfers between devices, all_to_all(jnp.stack([array_here for _ in range(axis_size(SEQ))], axis=0)...  11.7 us
  transfers between devices with their start and end apart: 35, of which 13 were waited for; matrix products, arithmetic and copies ran while one was open for 7% of the time, Pallas kernels for 0%

profile of v1, /device:TPU:8, one launch (start us, length us, event | category | flops | bytes accessed | tf_op | source)
XLA Modules:
  0.0 429.4 jit_solution(1620267550536280314)
XLA Ops:
  6.5 1.1 copy.31
  7.6 2.4 stack.22
  10.0 11.7 %all-to-all-start = ((bf16[16,512,256]{1,2,0:T(8,128)(2,1)}), bf16[16,512,256]{1,2,0:T(8,128)(2,1)}, u32[]{:S(2)}, u32[]{:S(2)}) async-start(bf16[16,512,256]{1,2,0:T(8,128)(2,1)} %stack.22), calls=%async_computation | async-start | bytes 8388608 | tf_op jit(solution)/shard_map/all_to_all | solution.py:12
  21.8 0.7 all-gather.2.cloned.1.call-update
  26.0 2.0 collective-permute-start.6
  28.1 1.1 reduce-window.26
  29.7 1.3 collective-permute-start
  31.0 0.9 fusion.53
  32.0 0.7 collective-permute-start.7
  32.9 1.2 fusion.5
  34.8 0.7 collective-permute-start.2
  35.5 0.7 collective-permute-start.8
  36.2 0.7 collective-permute-start.5
  36.8 0.7 collective-permute-start.4
  37.5 0.7 collective-permute-start.3
  38.3 0.7 collective-permute-start.11
  39.0 0.7 collective-permute-start.10
  39.7 0.7 collective-permute-start.9
  40.6 0.7 collective-permute-start.12
  41.7 0.7 compare_reduce_fusion.1
  42.4 0.7 compare_reduce_fusion
  43.1 1.7 convolution_bitcast_fusion.3
  44.9 0.8 collective-permute-start.13
  45.7 1.3 collective-permute-start.14
  47.1 0.7 fusion.4
  47.8 102.8 %collective-permute-done.14 = f32[8,64,128]{2,1,0:T(8,128)S(1)} collective-permute-done((f32[8,64,128]{2,1,0:T(8,128)S(1)}, f32[8,64,128]{2,1,0:T(8,128)S(1)}, u32[]{:S(2)}, u32[]{:S(2)}) %collective-permute-start.14) | collective-permute-done | bytes 262176 | tf_op jit(solution)/shard_map/ppermute | solution.py:68
  150.6 0.8 fusion.2
  151.8 0.7 copy-done.5
  153.0 1.3 fusion.40
  154.8 4.7 %convolution_convert_fusion.1 = bf16[512,4096]{1,0:T(8,128)(2,1)S(1)} fusion(bf16[512,4096]{0,1:T(8,128)(2,1)} %bitcast.26, f32[512]{0:T(512)S(1)} %copy-done.18, f32[512,512]{1,0:T(8,128)S(1)} %copy.30, bf16[512,512]{1,0:T(8,128)(2,1)S(1)} %copy-done.5), kind=kOutput, calls=%fused_computation.3 | convolution fusion | flops 2151677952 | bytes 9963520 | tf_op jit(solution)/shard_map/dot_general | solution.py:213
  160.3 2.8 collective-permute-start.18
  163.5 12.3 %collective-permute-done.18 = bf16[4,16,4224]{2,1,0:T(8,128)(2,1)S(1)} collective-permute-done((bf16[4,16,4224]{2,1,0:T(8,128)(2,1)S(1)}, bf16[4,16,4224]{2,1,0:T(8,128)(2,1)S(1)}, u32[]{:S(2)}, u32[]{:S(2)}) %collective-permute-start.18) | collective-permute-done | bytes 540704 | tf_op jit(solution)/shard_map/ppermute | solution.py:115
  175.9 3.8 collective-permute-start.19
  179.9 11.6 %collective-permute-done.19 = bf16[4,16,4224]{2,1,0:T(8,128)(2,1)S(1)} collective-permute-done((bf16[4,16,4224]{2,1,0:T(8,128)(2,1)S(1)}, bf16[4,16,4224]{2,1,0:T(8,128)(2,1)S(1)}, u32[]{:S(2)}, u32[]{:S(2)}) %collective-permute-start.19) | collective-permute-done | bytes 540704 | tf_op jit(solution)/shard_map/ppermute | solution.py:115
  191.7 3.8 collective-permute-start.20
  195.7 10.7 %collective-permute-done.20 = bf16[4,16,4224]{2,1,0:T(8,128)(2,1)S(1)} collective-permute-done((bf16[4,16,4224]{2,1,0:T(8,128)(2,1)S(1)}, bf16[4,16,4224]{2,1,0:T(8,128)(2,1)S(1)}, u32[]{:S(2)}, u32[]{:S(2)}) %collective-permute-start.20) | collective-permute-done | bytes 540704 | tf_op jit(solution)/shard_map/ppermute | solution.py:115
  206.6 3.5 collective-permute-done.17
  210.3 53.2 %all_to_all.20 = bf16[4,32,4224]{2,1,0:T(8,128)(2,1)S(1)} all-to-all(bf16[4,32,4224]{2,1,0:T(8,128)(2,1)S(1)} %pad_maximum_fusion.4), channel_id=1, replica_groups=mesh['sy'=4,'sz'=2,'sc'=2,'hx'=4,'hz'=4] {'hz'}, dimensions={0} | all-to-all | bytes 2162688 | tf_op jit(solution)/shard_map/all_to_all | solution.py:126
  264.5 27.5 %all_to_all.21 = bf16[4,32,4096]{2,1,0:T(8,128)(2,1)S(1)} all-to-all(bf16[4,32,4096]{2,1,0:T(8,128)(2,1)S(1)} %broadcast_in_dim.42), channel_id=1, replica_groups=mesh['sy'=4,'sz'=2,'sc'=2,'hx'=4,'hz'=4] {'hz'}, dimensions={0} | all-to-all | bytes 2097152 | tf_op jit(solution)/shard_map/all_to_all | solution.py:149
  292.6 1.5 collective-permute-start.21
  294.1 10.4 %collective-permute-done.24 = bf16[64,4096]{1,0:T(8,128)(2,1)S(1)} collective-permute-done((bf16[64,4096]{1,0:T(8,128)(2,1)S(1)}, bf16[64,4096]{1,0:T(8,128)(2,1)S(1)}, u32[]{:S(2)}, u32[]{:S(2)}) %collective-permute-start.24) | collective-permute-done | bytes 524320 | tf_op jit(solution)/shard_map/ppermute | solution.py:140
  304.5 1.7 collective-permute-start.25
  306.5 9.9 %collective-permute-done.25 = bf16[64,4096]{1,0:T(8,128)(2,1)S(1)} collective-permute-done((bf16[64,4096]{1,0:T(8,128)(2,1)S(1)}, bf16[64,4096]{1,0:T(8,128)(2,1)S(1)}, u32[]{:S(2)}, u32[]{:S(2)}) %collective-permute-start.25) | collective-permute-done | bytes 524320 | tf_op jit(solution)/shard_map/ppermute | solution.py:140
  316.5 2.5 collective-permute-start.26
  319.4 7.9 %collective-permute-done.26 = bf16[64,4096]{1,0:T(8,128)(2,1)S(1)} collective-permute-done((bf16[64,4096]{1,0:T(8,128)(2,1)S(1)}, bf16[64,4096]{1,0:T(8,128)(2,1)S(1)}, u32[]{:S(2)}, u32[]{:S(2)}) %collective-permute-start.26) | collective-permute-done | bytes 524320 | tf_op jit(solution)/shard_map/ppermute | solution.py:140
  327.5 2.0 gather_fusion.1
  329.5 3.2 broadcast_select_fusion
  332.8 1.5 pad_maximum_fusion.2
  334.2 2.0 gather_fusion
  336.3 2.0 broadcast_select_fusion.1
  339.0 2.1 copy-done.1
  341.1 1.1 copy-done.17
  342.2 2.3 fusion.74
  344.5 11.2 %convolution_convert_fusion = bf16[512,4096]{1,0:T(8,128)(2,1)} fusion(bf16[512,4096]{1,0:T(8,128)(2,1)} %all-gather.2.cloned.1.call-done, bf16[512,4096]{1,0:T(8,128)(2,1)} %bitcast.129, bf16[4096,512]{1,0:T(8,128)(2,1)} %param.36, f32[512,512]{1,0:T(8,128)S(1)} %fusion.74), kind=kOutput, calls=%fused_computation.2 | convolution fusion | flops 4298637312 | bytes 17825792 | tf_op jit(solution)/shard_map/dot_general | solution.py:238
  355.8 2.7 fusion.71
  358.5 3.7 collective-permute-start.30
  362.4 8.0 %collective-permute-done.30 = bf16[4,16,4096]{2,1,0:T(8,128)(2,1)S(1)} collective-permute-done((bf16[4,16,4096]{2,1,0:T(8,128)(2,1)S(1)}, bf16[4,16,4096]{2,1,0:T(8,128)(2,1)S(1)}, u32[]{:S(2)}, u32[]{:S(2)}) %collective-permute-start.30) | collective-permute-done | bytes 524320 | tf_op jit(solution)/shard_map/ppermute | solution.py:115
  370.5 3.8 collective-permute-start.31
  374.6 8.4 %collective-permute-done.31 = bf16[4,16,4096]{2,1,0:T(8,128)(2,1)S(1)} collective-permute-done((bf16[4,16,4096]{2,1,0:T(8,128)(2,1)S(1)}, bf16[4,16,4096]{2,1,0:T(8,128)(2,1)S(1)}, u32[]{:S(2)}, u32[]{:S(2)}) %collective-permute-start.31) | collective-permute-done | bytes 524320 | tf_op jit(solution)/shard_map/ppermute | solution.py:115
  383.1 3.8 collective-permute-start.32
  387.4 6.2 %collective-permute-done.32 = bf16[4,16,4096]{2,1,0:T(8,128)(2,1)S(1)} collective-permute-done((bf16[4,16,4096]{2,1,0:T(8,128)(2,1)S(1)}, bf16[4,16,4096]{2,1,0:T(8,128)(2,1)S(1)}, u32[]{:S(2)}, u32[]{:S(2)}) %collective-permute-start.32) | collective-permute-done | bytes 524320 | tf_op jit(solution)/shard_map/ppermute | solution.py:115
  393.8 4.1 collective-permute-done.29
  398.1 23.5 %all_to_all.22 = bf16[4,32,4096]{2,1,0:T(8,128)(2,1)S(1)} all-to-all(bf16[4,32,4096]{2,1,0:T(8,128)(2,1)S(1)} %pad_maximum_fusion.5), channel_id=1, replica_groups=mesh['sy'=4,'sz'=2,'sc'=2,'hx'=4,'hz'=4] {'hz'}, dimensions={0} | all-to-all | bytes 2097152 | tf_op jit(solution)/shard_map/all_to_all | solution.py:126
  421.7 0.8 add_convert_fusion.12
  (148 shorter events, 14.2 us)
Async XLA Ops:
  10.0 12.5 %copy-start.19 = (f32[8]{0:T(128)S(1)}, f32[8]{0:T(128)}, u32[]{:S(2)}) copy-start(f32[8]{0:T(128)} %param.29) | copy-start | bytes 100
  10.0 12.5 %copy-start.14 = (f32[8,512]{1,0:T(8,128)S(1)}, f32[8,512]{1,0:T(8,128)}, u32[]{:S(2)}) copy-start(f32[8,512]{1,0:T(8,128)} %param.27) | copy-start | bytes 49156
  10.0 12.5 %copy-start.15 = (f32[8]{0:T(128)S(1)}, f32[8]{0:T(128)}, u32[]{:S(2)}) copy-start(f32[8]{0:T(128)} %param.28) | copy-start | bytes 100
  10.0 14.2 %copy-start.3 = (bf16[512,512]{1,0:T(8,128)(2,1)S(1)}, bf16[512,512]{1,0:T(8,128)(2,1)}, u32[]{:S(2)}) copy-start(bf16[512,512]{1,0:T(8,128)(2,1)} %param.24) | copy-start | bytes 1572868
  10.0 144.8 %all-to-all-start = ((bf16[16,512,256]{1,2,0:T(8,128)(2,1)}), bf16[16,512,256]{1,2,0:T(8,128)(2,1)}, u32[]{:S(2)}, u32[]{:S(2)}) async-start(bf16[16,512,256]{1,2,0:T(8,128)(2,1)} %stack.22), calls=%async_computation | async-start | bytes 8388608 | tf_op jit(solution)/shard_map/all_to_all | solution.py:12
  21.7 3.3 copy-start.4
  21.7 242.0 %all-gather.2.cloned.1.call-start = ((), (), s32[]{:S(2)}) async-start(), calls=%async_computation.4 | async-start | bytes 4456448 | tf_op jit(solution)/shard_map/all_gather | solution.py:180
  24.5 1.0 copy-start.9
  26.0 5.9 %collective-permute-start.6 = (f32[8,64,128]{2,1,0:T(8,128)S(1)}, f32[8,64,128]{2,1,0:T(8,128)S(1)}, u32[]{:S(2)}, u32[]{:S(2)}) collective-permute-start(f32[8,64,128]{2,1,0:T(8,128)S(1)} %fusion.6), channel_id=1, source_target_pairs={{0,16},{32,48},{1,17},{33,49},{2,18},{34,50},{3,19},{35,51},{4,20}... | collective-permute-start | bytes 786440 | tf_op jit(solution)/shard_map/ppermute | solution.py:68
  29.7 4.4 %collective-permute-start = (f32[8]{0:T(128)S(1)}, f32[8]{0:T(128)S(1)}, u32[]{:S(2)}, u32[]{:S(2)}) collective-permute-start(f32[8]{0:T(128)S(1)} %fusion.61), channel_id=1, source_target_pairs={{0,16},{32,48},{1,17},{33,49},{2,18},{34,50},{3,19},{35,51},{4,20}... | collective-permute-start | bytes 104 | tf_op jit(solution)/shard_map/ppermute | solution.py:68
  32.0 3.4 collective-permute-start.7
  34.1 0.7 collective-permute-start.1
  34.8 1.4 collective-permute-start.2
  35.5 6.0 %copy-start.10 = (f32[8,64,128]{2,1,0:T(8,128)}, f32[8,64,128]{2,1,0:T(8,128)S(1)}, u32[]{:S(2)}) copy-start(f32[8,64,128]{2,1,0:T(8,128)S(1)} %collective-permute-done.7) | copy-start | bytes 786436
  35.5 2.7 collective-permute-start.8
  36.2 2.0 collective-permute-start.5
  36.8 3.5 collective-permute-start.4
  37.5 2.9 collective-permute-start.3
  38.3 2.1 collective-permute-start.11
  39.0 1.4 collective-permute-start.10
  39.7 0.8 collective-permute-start.9
  40.6 5.1 %collective-permute-start.12 = (f32[8,64,128]{2,1,0:T(8,128)S(1)}, f32[8,64,128]{2,1,0:T(8,128)S(1)}, u32[]{:S(2)}, u32[]{:S(2)}) collective-permute-start(f32[8,64,128]{2,1,0:T(8,128)S(1)} %select_add_fusion), channel_id=1, source_target_pairs={{48,16},{49,17},{50,18},{51,19},{52,20},{53,21},{54,22},{55,23},{5... | collective-permute-start | bytes 786440 | tf_op jit(solution)/shard_map/ppermute | solution.py:68
  41.7 5.3 %copy-start.6 = (f32[256,8,64]{0,2,1:T(8,128)S(1)}, f32[256,8,64]{0,2,1:T(8,128)}, u32[]{:S(2)}) copy-start(f32[256,8,64]{0,2,1:T(8,128)} %fusion.5) | copy-start | bytes 1572868
  44.9 105.7 %copy-start.11 = (f32[8,64,128]{2,1,0:T(8,128)S(1)}, f32[8,64,128]{2,1,0:T(8,128)}, u32[]{:S(2)}) copy-start(f32[8,64,128]{2,1,0:T(8,128)} %copy-done.10) | copy-start | bytes 786436
  44.9 105.7 %copy-start.16 = (f32[8]{0:T(128)S(1)}, f32[8]{0:T(128)}, u32[]{:S(2)}) copy-start(f32[8]{0:T(128)} %param.30) | copy-start | bytes 100
  44.9 2.9 collective-permute-start.13
  45.7 104.9 %copy-start.12 = (f32[8,64,128]{2,1,0:T(8,128)}, f32[8,64,128]{2,1,0:T(8,128)S(1)}, u32[]{:S(2)}) copy-start(f32[8,64,128]{2,1,0:T(8,128)S(1)} %collective-permute-done.12) | copy-start | bytes 786436
  45.7 104.8 %collective-permute-start.14 = (f32[8,64,128]{2,1,0:T(8,128)S(1)}, f32[8,64,128]{2,1,0:T(8,128)S(1)}, u32[]{:S(2)}, u32[]{:S(2)}) collective-permute-start(f32[8,64,128]{2,1,0:T(8,128)S(1)} %collective-permute-done.12), channel_id=1, source_target_pairs={{16,0},{17,1},{18,2},{19,3},{20,4},{21,5},{22,6},{23,7},{24,8},{25... | collective-permute-start | bytes 786440 | tf_op jit(solution)/shard_map/ppermute | solution.py:68
  151.4 1.0 copy-start.5
  151.4 3.4 copy-start.18
  160.3 15.4 %collective-permute-start.18 = (bf16[4,16,4224]{2,1,0:T(8,128)(2,1)S(1)}, bf16[4,16,4224]{2,1,0:T(8,128)(2,1)S(1)}, u32[]{:S(2)}, u32[]{:S(2)}) collective-permute-start(bf16[4,16,4224]{2,1,0:T(8,128)(2,1)S(1)} %select_bitcast_fusion), channel_id=1, source_target_pairs={{0,12},{4,0},{8,4},{12,8},{1,13},{5,1},{9,5},{13,9},{2,14},{6,2},{... | collective-permute-start | bytes 1622024 | tf_op jit(solution)/shard_map/ppermute | solution.py:115
  163.2 16.5 %collective-permute-start.15 = (bf16[4,16,4224]{2,1,0:T(8,128)(2,1)S(1)}, bf16[4,16,4224]{2,1,0:T(8,128)(2,1)S(1)}, u32[]{:S(2)}, u32[]{:S(2)}) collective-permute-start(bf16[4,16,4224]{2,1,0:T(8,128)(2,1)S(1)} %select_bitcast_fusion.1), channel_id=1, source_target_pairs={{0,4},{4,8},{8,12},{12,0},{1,5},{5,9},{9,13},{13,1},{2,6},{6,10},{... | collective-permute-start | bytes 1622024 | tf_op jit(solution)/shard_map/ppermute | solution.py:115
  175.9 15.6 %collective-permute-start.19 = (bf16[4,16,4224]{2,1,0:T(8,128)(2,1)S(1)}, bf16[4,16,4224]{2,1,0:T(8,128)(2,1)S(1)}, u32[]{:S(2)}, u32[]{:S(2)}) collective-permute-start(bf16[4,16,4224]{2,1,0:T(8,128)(2,1)S(1)} %add_convert_fusion.2), channel_id=1, source_target_pairs={{0,12},{4,0},{8,4},{12,8},{1,13},{5,1},{9,5},{13,9},{2,14},{6,2},{... | collective-permute-start | bytes 1622024 | tf_op jit(solution)/shard_map/ppermute | solution.py:115
  179.9 15.6 %collective-permute-start.16 = (bf16[4,16,4224]{2,1,0:T(8,128)(2,1)S(1)}, bf16[4,16,4224]{2,1,0:T(8,128)(2,1)S(1)}, u32[]{:S(2)}, u32[]{:S(2)}) collective-permute-start(bf16[4,16,4224]{2,1,0:T(8,128)(2,1)S(1)} %add_convert_fusion.5), channel_id=1, source_target_pairs={{0,4},{4,8},{8,12},{12,0},{1,5},{5,9},{9,13},{13,1},{2,6},{6,10},{... | collective-permute-start | bytes 1622024 | tf_op jit(solution)/shard_map/ppermute | solution.py:115
  191.7 14.7 %collective-permute-start.20 = (bf16[4,16,4224]{2,1,0:T(8,128)(2,1)S(1)}, bf16[4,16,4224]{2,1,0:T(8,128)(2,1)S(1)}, u32[]{:S(2)}, u32[]{:S(2)}) collective-permute-start(bf16[4,16,4224]{2,1,0:T(8,128)(2,1)S(1)} %add_convert_fusion.1), channel_id=1, source_target_pairs={{0,12},{4,0},{8,4},{12,8},{1,13},{5,1},{9,5},{13,9},{2,14},{6,2},{... | collective-permute-start | bytes 1622024 | tf_op jit(solution)/shard_map/ppermute | solution.py:115
  195.6 14.4 %collective-permute-start.17 = (bf16[4,16,4224]{2,1,0:T(8,128)(2,1)S(1)}, bf16[4,16,4224]{2,1,0:T(8,128)(2,1)S(1)}, u32[]{:S(2)}, u32[]{:S(2)}) collective-permute-start(bf16[4,16,4224]{2,1,0:T(8,128)(2,1)S(1)} %add_convert_fusion.4), channel_id=1, source_target_pairs={{0,4},{4,8},{8,12},{12,0},{1,5},{5,9},{9,13},{13,1},{2,6},{6,10},{... | collective-permute-start | bytes 1622024 | tf_op jit(solution)/shard_map/ppermute | solution.py:115
  210.3 53.6 %copy-start.2 = (bf16[32,4096]{1,0:T(8,128)(2,1)S(1)}, bf16[32,4096]{1,0:T(8,128)(2,1)}, u32[]{:S(2)}) copy-start(bf16[32,4096]{1,0:T(8,128)(2,1)} %param.33) | copy-start | bytes 786436
  210.3 53.9 %copy-start.13 = (f32[4096]{0:T(1024)S(1)}, f32[4096]{0:T(1024)}, u32[]{:S(2)}) copy-start(f32[4096]{0:T(1024)} %param.34) | copy-start | bytes 49156
  292.0 12.5 %collective-permute-start.24 = (bf16[64,4096]{1,0:T(8,128)(2,1)S(1)}, bf16[64,4096]{1,0:T(8,128)(2,1)S(1)}, u32[]{:S(2)}, u32[]{:S(2)}) collective-permute-start(bf16[64,4096]{1,0:T(8,128)(2,1)S(1)} %bitcast.134), channel_id=1, source_target_pairs={{0,12},{4,0},{8,4},{12,8},{1,13},{5,1},{9,5},{13,9},{2,14},{6,2},{... | collective-permute-start | bytes 1572872 | tf_op jit(solution)/shard_map/ppermute | solution.py:140
  292.6 13.6 %collective-permute-start.21 = (bf16[64,4096]{1,0:T(8,128)(2,1)S(1)}, bf16[64,4096]{1,0:T(8,128)(2,1)S(1)}, u32[]{:S(2)}, u32[]{:S(2)}) collective-permute-start(bf16[64,4096]{1,0:T(8,128)(2,1)S(1)} %bitcast.132), channel_id=1, source_target_pairs={{0,4},{4,8},{8,12},{12,0},{1,5},{5,9},{9,13},{13,1},{2,6},{6,10},{... | collective-permute-start | bytes 1572872 | tf_op jit(solution)/shard_map/ppermute | solution.py:140
  304.5 12.0 %collective-permute-start.25 = (bf16[64,4096]{1,0:T(8,128)(2,1)S(1)}, bf16[64,4096]{1,0:T(8,128)(2,1)S(1)}, u32[]{:S(2)}, u32[]{:S(2)}) collective-permute-start(bf16[64,4096]{1,0:T(8,128)(2,1)S(1)} %collective-permute-done.24), channel_id=1, source_target_pairs={{0,12},{4,0},{8,4},{12,8},{1,13},{5,1},{9,5},{13,9},{2,14},{6,2},{... | collective-permute-start | bytes 1572872 | tf_op jit(solution)/shard_map/ppermute | solution.py:140
  306.2 21.1 %copy-start.7 = (bf16[64,4096]{1,0:T(8,128)(2,1)}, bf16[64,4096]{1,0:T(8,128)(2,1)S(1)}, u32[]{:S(2)}) copy-start(bf16[64,4096]{1,0:T(8,128)(2,1)S(1)} %collective-permute-done.21) | copy-start | bytes 1572868
  306.2 12.8 %collective-permute-start.22 = (bf16[64,4096]{1,0:T(8,128)(2,1)S(1)}, bf16[64,4096]{1,0:T(8,128)(2,1)}, u32[]{:S(2)}, u32[]{:S(2)}) collective-permute-start(bf16[64,4096]{1,0:T(8,128)(2,1)S(1)} %collective-permute-done.21), channel_id=1, source_target_pairs={{0,4},{4,8},{8,12},{12,0},{1,5},{5,9},{9,13},{13,1},{2,6},{6,10},{... | collective-permute-start | bytes 1572872 | tf_op jit(solution)/shard_map/ppermute | solution.py:140
  316.5 10.8 %collective-permute-start.26 = (bf16[64,4096]{1,0:T(8,128)(2,1)S(1)}, bf16[64,4096]{1,0:T(8,128)(2,1)S(1)}, u32[]{:S(2)}, u32[]{:S(2)}) collective-permute-start(bf16[64,4096]{1,0:T(8,128)(2,1)S(1)} %collective-permute-done.25), channel_id=1, source_target_pairs={{0,12},{4,0},{8,4},{12,8},{1,13},{5,1},{9,5},{13,9},{2,14},{6,2},{... | collective-permute-start | bytes 1572872 | tf_op jit(solution)/shard_map/ppermute | solution.py:140
  319.0 13.7 %collective-permute-start.23 = (bf16[64,4096]{1,0:T(8,128)(2,1)}, bf16[64,4096]{1,0:T(8,128)(2,1)}, u32[]{:S(2)}, u32[]{:S(2)}) collective-permute-start(bf16[64,4096]{1,0:T(8,128)(2,1)} %collective-permute-done.22), channel_id=1, source_target_pairs={{0,4},{4,8},{8,12},{12,0},{1,5},{5,9},{9,13},{13,1},{2,6},{6,10},{... | collective-permute-start | bytes 1572872 | tf_op jit(solution)/shard_map/ppermute | solution.py:140
  329.5 3.2 copy-start.8
  336.3 2.2 copy-start
  338.5 3.7 copy-start.17
  339.0 2.1 copy-start.1
  358.5 11.8 %collective-permute-start.30 = (bf16[4,16,4096]{2,1,0:T(8,128)(2,1)S(1)}, bf16[4,16,4096]{2,1,0:T(8,128)(2,1)S(1)}, u32[]{:S(2)}, u32[]{:S(2)}) collective-permute-start(bf16[4,16,4096]{2,1,0:T(8,128)(2,1)S(1)} %select_bitcast_fusion.2), channel_id=1, source_target_pairs={{0,12},{4,0},{8,4},{12,8},{1,13},{5,1},{9,5},{13,9},{2,14},{6,2},{... | collective-permute-start | bytes 1572872 | tf_op jit(solution)/shard_map/ppermute | solution.py:115
  362.3 12.0 %collective-permute-start.27 = (bf16[4,16,4096]{2,1,0:T(8,128)(2,1)S(1)}, bf16[4,16,4096]{2,1,0:T(8,128)(2,1)S(1)}, u32[]{:S(2)}, u32[]{:S(2)}) collective-permute-start(bf16[4,16,4096]{2,1,0:T(8,128)(2,1)S(1)} %select_bitcast_fusion.3), channel_id=1, source_target_pairs={{0,4},{4,8},{8,12},{12,0},{1,5},{5,9},{9,13},{13,1},{2,6},{6,10},{... | collective-permute-start | bytes 1572872 | tf_op jit(solution)/shard_map/ppermute | solution.py:115
  370.5 12.4 %collective-permute-start.31 = (bf16[4,16,4096]{2,1,0:T(8,128)(2,1)S(1)}, bf16[4,16,4096]{2,1,0:T(8,128)(2,1)S(1)}, u32[]{:S(2)}, u32[]{:S(2)}) collective-permute-start(bf16[4,16,4096]{2,1,0:T(8,128)(2,1)S(1)} %add_convert_fusion.8), channel_id=1, source_target_pairs={{0,12},{4,0},{8,4},{12,8},{1,13},{5,1},{9,5},{13,9},{2,14},{6,2},{... | collective-permute-start | bytes 1572872 | tf_op jit(solution)/shard_map/ppermute | solution.py:115
  374.5 12.7 %collective-permute-start.28 = (bf16[4,16,4096]{2,1,0:T(8,128)(2,1)S(1)}, bf16[4,16,4096]{2,1,0:T(8,128)(2,1)S(1)}, u32[]{:S(2)}, u32[]{:S(2)}) collective-permute-start(bf16[4,16,4096]{2,1,0:T(8,128)(2,1)S(1)} %add_convert_fusion.11), channel_id=1, source_target_pairs={{0,4},{4,8},{8,12},{12,0},{1,5},{5,9},{9,13},{13,1},{2,6},{6,10},{... | collective-permute-start | bytes 1572872 | tf_op jit(solution)/shard_map/ppermute | solution.py:115
  383.1 10.5 %collective-permute-start.32 = (bf16[4,16,4096]{2,1,0:T(8,128)(2,1)S(1)}, bf16[4,16,4096]{2,1,0:T(8,128)(2,1)S(1)}, u32[]{:S(2)}, u32[]{:S(2)}) collective-permute-start(bf16[4,16,4096]{2,1,0:T(8,128)(2,1)S(1)} %add_convert_fusion.7), channel_id=1, source_target_pairs={{0,12},{4,0},{8,4},{12,8},{1,13},{5,1},{9,5},{13,9},{2,14},{6,2},{... | collective-permute-start | bytes 1572872 | tf_op jit(solution)/shard_map/ppermute | solution.py:115
  387.3 10.5 %collective-permute-start.29 = (bf16[4,16,4096]{2,1,0:T(8,128)(2,1)S(1)}, bf16[4,16,4096]{2,1,0:T(8,128)(2,1)S(1)}, u32[]{:S(2)}, u32[]{:S(2)}) collective-permute-start(bf16[4,16,4096]{2,1,0:T(8,128)(2,1)S(1)} %add_convert_fusion.10), channel_id=1, source_target_pairs={{0,4},{4,8},{8,12},{12,0},{1,5},{5,9},{9,13},{13,1},{2,6},{6,10},{... | collective-permute-start | bytes 1572872 | tf_op jit(solution)/shard_map/ppermute | solution.py:115
Sparse Core Ops, SparseCore 0:
  25.1 141.3 all-gather.1
